TPU v7x, 512 devices: a whole 4x8x8 slice. The times are simulated.
512 devices in a mesh: tiles: 128 (over z, y, core), rep: 4 (over x).
Axes of the slice: x: 4, y: 8, z: 8, core: 2. Of those that a mesh axis runs over, the one named last changes fastest.
Arguments:
- tile_data: float32 [1536, 64, 4096], P(('tiles', 'rep')), may hold values from -64 to 64
- tile_coords: int32 [1536, 3], P(('tiles', 'rep')), may hold values from 0 to 127, as said below
- tile_count: int32 [512], P(('tiles', 'rep')), may hold values from 1 to 3, 1024 in all
- weights: int32 [1536], P(('tiles', 'rep')), may hold values from 1 to 4
- owner_map: int32 [128], replicated, may hold values from 0 to 127, as said below
- factor_b: bfloat16 [8192, 256], P(('tiles', 'rep'))
- factor_c: bfloat16 [1024, 256], replicated
Outputs:
- updated: float32 [8192, 256], P(('tiles', 'rep'))
Inputs may be any that keep to these rules, and one draw needn't show every extreme that they name: `tile_coords`: columns 0 and 1 name row blocks below 128, column 2 a block below 16. Every slot of device d = t * 4 + e has owner_map[i_s] = t. Among the 3 slots of one device the positions owner_map[j_s] all differ. `owner_map`: A permutation of the 128 row blocks.
All inputs are finite; a program needn't handle non-finite values. No bound on the sum of `tile_count` on one device may be relied on, other than what follows from the above.
Results may differ from a plain program's by a relative error of at most 0.0095.
Values may be sent and summed in bfloat16 or wider, within the bound.
No kernel may reach another device: no remote copies, remote signals or barrier semaphores. Data moves between devices by JAX's collectives and lax.ppermute only.
A program may use at most 128 MiB of HBM per device.

v0:
```python
import jax
import jax.numpy as jnp
from jax import lax
from jax.sharding import PartitionSpec as P


def per_device(tile_data, tile_coords, tile_count, weights, owner_map, factor_b, factor_c):
    slot_total = tile_data.shape[0]
    tile_edge = tile_data.shape[1]
    rank_cols = factor_b.shape[1]
    is_live = jnp.arange(slot_total, dtype=jnp.int32) < tile_count[0]
    slot_scale = weights.astype(jnp.float32) * is_live.astype(jnp.float32)
    stored_second = jnp.take(owner_map, tile_coords[:, 1])
    block_offsets = jnp.arange(tile_edge, dtype=jnp.int32)
    initial = jnp.zeros((slot_total, tile_edge, rank_cols), jnp.bfloat16)
    owned = lax.all_gather(factor_b, "rep", axis=0, tiled=True)
    row_piece = lax.all_gather(owned, "tiles", axis=0, tiled=True)
    piece_rows = row_piece.shape[0]
    wanted = stored_second[:, None] * tile_edge + block_offsets[None, :]
    inside = (wanted >= 0) & (wanted < piece_rows)
    taken = jnp.take(row_piece, jnp.clip(wanted, 0, piece_rows - 1), axis=0)
    blocks = jnp.where(inside[:, :, None], taken, initial)
    summed = jnp.zeros((tile_edge, rank_cols), jnp.float32)
    for position in range(slot_total):
        c_block = lax.dynamic_slice_in_dim(
            factor_c, tile_coords[position, 2] * tile_edge, tile_edge, 0
        ).astype(jnp.float32)
        flat_tile = tile_data[position].reshape(tile_edge * tile_edge, tile_edge)
        inner_sum = jnp.dot(flat_tile, c_block, precision=lax.Precision.HIGHEST)
        inner_sum = inner_sum.reshape(tile_edge, tile_edge, rank_cols)
        partial_value = jnp.einsum("ijr,jr->ir", inner_sum, blocks[position].astype(jnp.float32))
        rounded = (partial_value * slot_scale[position]).astype(jnp.bfloat16)
        summed = summed + rounded.astype(jnp.float32)
    my_rows = lax.psum_scatter(summed, "rep", scatter_dimension=0, tiled=True)
    own_gram = jnp.dot(factor_b.T, factor_b, preferred_element_type=jnp.float32)
    gram_b = lax.psum(own_gram, ("tiles", "rep"))
    gram_c = jnp.dot(factor_c.T, factor_c, preferred_element_type=jnp.float32)
    normal_matrix = gram_b * gram_c
    lower_factor = jnp.linalg.cholesky(normal_matrix)
    return jax.scipy.linalg.cho_solve((lower_factor, True), my_rows.T).T


def solution(mesh):
    in_specs = (
        P(("tiles", "rep"), None, None),
        P(("tiles", "rep"), None),
        P(("tiles", "rep")),
        P(("tiles", "rep")),
        P(),
        P(("tiles", "rep"), None),
        P(),
    )
    out_specs = P(("tiles", "rep"), None)
    return jax.shard_map(
        per_device, mesh=mesh, in_specs=in_specs, out_specs=out_specs, check_vma=False
    )
```

profile of v0, /device:TPU:23, one launch (start us, length us, event | category | flops | bytes accessed | tf_op | source)
XLA Modules:
  0.0 374.4 jit_solution(15148988416922388078)
XLA Ops:
  7.4 1.7 fusion.28
  9.1 10.0 %all_gather.6 = bf16[64,256]{1,0:T(8,128)(2,1)} all-gather(bf16[16,256]{1,0:T(8,128)(2,1)} %param.12), channel_id=1, replica_groups=mesh['tiles'=128,'rep'=4] {'rep'}, dimensions={0}, use_global_device_ids=true | all-gather | bytes 40960 | tf_op jit(solution)/shard_map/all_gather | solution.py:16
  19.2 0.8 slice.101
  19.9 1.5 fusion.26
  23.4 0.1 copy.55
  23.5 1.3 gather_fusion
  25.0 3.7 fusion.25
  28.7 2.0 reshape_squeeze.9
  30.7 3.9 %convolution_bitcast_fusion.2 = f32[4096,256]{0,1:T(8,128)} fusion(f32[4096,64]{1,0:T(8,128)S(1)} %reshape_squeeze.9, bf16[1024,256]{1,0:T(8,128)(2,1)S(1)} %copy-done, s32[]{:T(128)S(6)} %select_n.56), kind=kOutput, calls=%fused_computation.6 | convolution fusion | flops 805306368 | bytes 6324228 | tf_op jit(solution)/shard_map/dot_general | solution.py:29
  34.7 5.6 %copy.50 = f32[4096,256]{1,0:T(8,128)} copy(f32[4096,256]{0,1:T(8,128)} %convolution_bitcast_fusion.2) | data formatting | bytes 8388608
  40.3 2.0 reshape_squeeze.11
  42.3 3.9 %convolution_bitcast_fusion = f32[4096,256]{0,1:T(8,128)} fusion(f32[4096,64]{1,0:T(8,128)S(1)} %reshape_squeeze.11, bf16[1024,256]{1,0:T(8,128)(2,1)S(1)} %copy-done, s32[]{:T(128)S(6)} %select_n.58), kind=kOutput, calls=%fused_computation.4 | convolution fusion | flops 805306368 | bytes 6324228 | tf_op jit(solution)/shard_map/dot_general | solution.py:29
  46.2 5.6 %copy.52 = f32[4096,256]{1,0:T(8,128)} copy(f32[4096,256]{0,1:T(8,128)} %convolution_bitcast_fusion) | data formatting | bytes 8388608
  51.8 2.0 reshape_squeeze.10
  53.8 3.9 %convolution_bitcast_fusion.1 = f32[4096,256]{0,1:T(8,128)} fusion(f32[4096,64]{1,0:T(8,128)S(1)} %reshape_squeeze.10, bf16[1024,256]{1,0:T(8,128)(2,1)S(1)} %copy-done, s32[]{:T(128)S(6)} %select_n.57), kind=kOutput, calls=%fused_computation.5 | convolution fusion | flops 805306368 | bytes 6324228 | tf_op jit(solution)/shard_map/dot_general | solution.py:29
  57.7 5.7 %copy.51 = f32[4096,256]{1,0:T(8,128)} copy(f32[4096,256]{0,1:T(8,128)} %convolution_bitcast_fusion.1) | data formatting | bytes 8388608
  64.1 0.7 fusion.27
  64.8 223.5 %all-reduce.3.cloned.1.call-done = f32[256,256]{0,1:T(8,128)} async-done(((f32[256,256]{0,1:T(8,128)}), f32[256,256]{0,1:T(8,128)}) %all-reduce.3.cloned.1.call-update) | async-done | bytes 262160 | tf_op jit(solution)/shard_map/psum | solution.py:36
  288.3 1.3 convolution_multiply_fusion
  289.6 0.1 copy.21
  289.8 11.7 %cholesky.50 = f32[128,128]{1,0:T(8,128)S(1)} custom-call(f32[128,128]{1,0:T(8,128)S(1)} %cholesky.118), custom_call_target="Cholesky" | custom-call | tf_op jit(solution)/shard_map/jit(cholesky)/cholesky | solution.py:39
  301.5 9.8 %custom-call.18 = f32[1,128,128]{1,2,0:T(8,128)S(1)} custom-call(f32[1,128,128]{2,1,0:T(8,128)S(1)} %get-tuple-element.32), custom_call_target="InvertDiagBlocksLowerTriangular" | custom-call | tf_op jit(solution)/shard_map/jit(cholesky)/cholesky | solution.py:39
  311.4 0.2 constant_dynamic-update-slice_fusion
  311.6 0.3 convolution_subtract_fusion
  311.8 11.7 %cholesky.105 = f32[128,128]{1,0:T(8,128)S(1)} custom-call(f32[128,128]{1,0:T(8,128)S(1)} %convolution_subtract_fusion), custom_call_target="Cholesky" | custom-call | tf_op jit(solution)/shard_map/jit(cholesky)/cholesky | solution.py:39
  323.6 0.7 compare_reduce_fusion
  325.6 3.6 gather_fusion.1
  329.2 0.1 select_select_fusion.1
  329.3 3.0 multiply_reduce_fusion.2
  332.4 0.1 copy.35
  332.5 4.9 %multiply_reduce_fusion = (f32[256,64]{0,1:T(8,128)S(1)}, f32[256,64]{0,1:T(8,128)S(1)}) fusion(f32[256,64]{0,1:T(8,128)S(1)} %get-tuple-element.26, f32[4096,256]{1,0:T(8,128)} %copy.52, f32[4096,256]{1,0:T(8,128)} %copy.51, f32[256,64]{0,1:T(8,128)S(1)} %get-tuple-element.27), kind=kLoop, calls=%fused_computation.7 | loop fusion | flops 4161536 | bytes 8650752
  337.4 0.1 copy.42
  337.5 0.1 copy.49
  337.6 1.9 add_bitcast_fusion
  339.5 0.7 copy.53
  340.3 3.8 %while.1 = (s32[]{:T(128)}, f32[256,256]{1,0:T(8,128)S(1)}, s32[2,2]{1,0:T(2,128)S(1)}, f32[2,128,128]{2,1,0:T(8,128)S(1)}, s32[]{:T(128)}) while((s32[]{:T(128)}, f32[256,256]{1,0:T(8,128)S(1)}, s32[2,2]{1,0:T(2,128)S(1)}, f32[2,128,128]{2,1,0:T(8,128)S(1)}, s32[]{:T(128)}) %tuple.33), condition=%wide.while_cond, body=%wide.while_body.sunk | while | flops 2 | bytes 131189 | solution.py:40
  340.3 0.6 fusion.44
  340.9 1.3 bitcast_dynamic-update-slice_fusion.2
  342.2 0.6 fusion.44
  342.8 1.3 bitcast_dynamic-update-slice_fusion.2
  344.1 19.7 %custom-call.19 = f32[2,128,128]{1,2,0:T(8,128)S(1)} custom-call(f32[2,128,128]{2,1,0:T(8,128)S(1)} %get-tuple-element.12), custom_call_target="InvertDiagBlocksLowerTriangular" | custom-call | tf_op jit(solution)/shard_map/jit(_cho_solve)/triangular_solve | solution.py:40
  363.8 0.9 fusion.5
  364.7 0.9 convolution_subtract_fusion.2
  365.5 0.2 fusion.7
  365.7 0.2 fusion.6
  365.9 0.2 convolution_subtract_fusion.1
  366.1 0.2 fusion.4
  366.3 0.7 maximum_bitcast_fusion
  (32 shorter events, 0.7 us)
Async XLA Ops:
  7.4 23.4 %copy-start = (bf16[1024,256]{1,0:T(8,128)(2,1)S(1)}, bf16[1024,256]{1,0:T(8,128)(2,1)}, u32[]{:S(2)}) copy-start(bf16[1024,256]{1,0:T(8,128)(2,1)} %param.13) | copy-start | bytes 1572868
  7.4 280.9 %all-reduce.3.cloned.1.call-start = ((), (), s32[]{:S(2)}) async-start(), calls=%async_computation.1 | async-start | bytes 524288 | tf_op jit(solution)/shard_map/psum | solution.py:36
  9.1 316.5 %all-gather.2.cloned.1.call-start = ((), (), s32[]{:S(2)}) async-start(), calls=%async_computation.2 | async-start | bytes 4227072 | tf_op jit(solution)/shard_map/all_gather | solution.py:17
  19.1 344.7 %reduce-scatter.4.cloned.1.call-start = ((), (), s32[]{:S(2)}) async-start(), calls=%async_computation.3 | async-start | bytes 81920 | tf_op jit(solution)/shard_map/reduce_scatter | solution.py:34
  57.7 6.3 %copy-start.1 = (s32[3]{0:T(128)S(1)}, s32[3]{0:T(128)}, u32[]{:S(2)}) copy-start(s32[3]{0:T(128)} %param.10) | copy-start | bytes 40
Sparse Core Ops, SparseCore 0:
  13.2 275.0 all-reduce.2
Sparse Core Ops, SparseCore 1:
  19.2 92.1 all-gather.1
  340.3 17.2 reduce-scatter.3
where the time goes:
time: 375 us; the launch traced here: 374 us
  waiting for transfers between devices  224 us (60%)
  other arithmetic  64.6 us (17%)
  local copies, waits for them, and re-layouts  39.5 us (11%)
  between operations  19 us (5%)
  matrix products  17.7 us (5%)
  blocking collectives  9.96 us (3%)
    psum x1, waiting for transfers between devices, per_device(): gram_b = lax.psum(own_gram, ('tiles', 'rep'))  223 us
    another operation x6, other arithmetic, per_device(): lower_factor = jnp.linalg.cholesky(normal_matrix)  34 us
    another operation x3, other arithmetic, per_device(): return jax.scipy.linalg.cho_solve((lower_factor, True), my_rows.T).T  19.7 us
    unnamed x9, local copies, waits for them, and re-layouts  17.7 us
    dot_general x3, matrix products, per_device(): inner_sum = jnp.dot(flat_tile, c_block, precision=lax.Precision.HIGHEST)  11.7 us
    all_gather x1, blocking collectives, per_device(): owned = lax.all_gather(factor_b, 'rep', axis=0, tiled=True)  9.96 us
    unnamed x4, other arithmetic  7.99 us
  transfers between devices with their start and end apart: 3, of which 1 were waited for; matrix products, arithmetic and copies ran while one was open for 27% of the time, Pallas kernels for 0%

commit v1 on v0

--- a/solution.py
+++ b/solution.py
@@ -2,6 +2,11 @@
 import jax.numpy as jnp
 from jax import lax
 from jax.sharding import PartitionSpec as P
+
+clear_chunk = lambda content, axis_tag: jnp.concatenate(
+    lax.all_to_all(jnp.stack([content for _ in range(lax.axis_size(axis_tag))]), axis_tag, 0, 0),
+    axis=0,
+)
 
 
 def per_device(tile_data, tile_coords, tile_count, weights, owner_map, factor_b, factor_c):
@@ -13,7 +18,7 @@
     stored_second = jnp.take(owner_map, tile_coords[:, 1])
     block_offsets = jnp.arange(tile_edge, dtype=jnp.int32)
     initial = jnp.zeros((slot_total, tile_edge, rank_cols), jnp.bfloat16)
-    owned = lax.all_gather(factor_b, "rep", axis=0, tiled=True)
+    owned = clear_chunk(factor_b, "rep")
     row_piece = lax.all_gather(owned, "tiles", axis=0, tiled=True)
     piece_rows = row_piece.shape[0]
     wanted = stored_second[:, None] * tile_edge + block_offsets[None, :]

time: 375 us -> 375 us (level)
    all_gather x1 -> x0, blocking collectives: 9.96 us -> none  [per_device(): owned = lax.all_gather(factor_b, 'rep', axis=0, tiled=True)]
    all_to_all x0 -> x1, blocking collectives: none -> 6.62 us  [lax.all_to_all(jnp.stack([content for _ in range(lax.axis_size(axis_tag))...]
  transfers between devices with their start and end apart: 3 -> 3, of which waited for: 1 -> 1; matrix products, arithmetic and copies ran while one was open for 27% -> 28% of each run, Pallas kernels for 0% -> 0%
where the time goes in v1:
time: 375 us; the launch traced here: 374 us
  waiting for transfers between devices  226 us (60%)
  other arithmetic  64.6 us (17%)
  local copies, waits for them, and re-layouts  40.2 us (11%)
  between operations  19 us (5%)
  matrix products  17.7 us (5%)
  blocking collectives  6.62 us (2%)
    psum x1, waiting for transfers between devices, per_device(): gram_b = lax.psum(own_gram, ('tiles', 'rep'))  226 us
    another operation x6, other arithmetic, per_device(): lower_factor = jnp.linalg.cholesky(normal_matrix)  34 us
    another operation x3, other arithmetic, per_device(): return jax.scipy.linalg.cho_solve((lower_factor, True), my_rows.T).T  19.7 us
    unnamed x9, local copies, waits for them, and re-layouts  17.7 us
    dot_general x3, matrix products, per_device(): inner_sum = jnp.dot(flat_tile, c_block, precision=lax.Precision.HIGHEST)  11.7 us
    unnamed x4, other arithmetic  7.99 us
  transfers between devices with their start and end apart: 3, of which 1 were waited for; matrix products, arithmetic and copies ran while one was open for 28% of the time, Pallas kernels for 0%

profile of v1, /device:TPU:23, one launch (start us, length us, event | category | flops | bytes accessed | tf_op | source)
XLA Modules:
  0.0 374.1 jit_solution(5239192876259579610)
XLA Ops:
  7.4 1.7 fusion.28
  9.1 0.7 stack.2
  9.8 6.6 %all_to_all.5 = bf16[4,16,256]{2,1,0:T(8,128)(2,1)} all-to-all(bf16[4,16,256]{2,1,0:T(8,128)(2,1)S(1)} %stack.2), channel_id=1, replica_groups=mesh['tiles'=128,'rep'=4] {'rep'}, dimensions={0} | all-to-all | bytes 65536 | tf_op jit(solution)/shard_map/all_to_all | solution.py:7
  16.6 0.8 slice.101
  17.3 1.5 fusion.26
  20.8 0.1 copy.55
  20.9 1.3 gather_fusion
  22.4 3.7 fusion.25
  26.1 2.0 reshape_squeeze.9
  28.1 3.9 %convolution_bitcast_fusion.2 = f32[4096,256]{0,1:T(8,128)} fusion(f32[4096,64]{1,0:T(8,128)S(1)} %reshape_squeeze.9, bf16[1024,256]{1,0:T(8,128)(2,1)S(1)} %copy-done, s32[]{:T(128)S(6)} %select_n.56), kind=kOutput, calls=%fused_computation.6 | convolution fusion | flops 805306368 | bytes 6324228 | tf_op jit(solution)/shard_map/dot_general | solution.py:34
  32.0 5.6 %copy.50 = f32[4096,256]{1,0:T(8,128)} copy(f32[4096,256]{0,1:T(8,128)} %convolution_bitcast_fusion.2) | data formatting | bytes 8388608
  37.6 2.0 reshape_squeeze.11
  39.7 3.9 %convolution_bitcast_fusion = f32[4096,256]{0,1:T(8,128)} fusion(f32[4096,64]{1,0:T(8,128)S(1)} %reshape_squeeze.11, bf16[1024,256]{1,0:T(8,128)(2,1)S(1)} %copy-done, s32[]{:T(128)S(6)} %select_n.58), kind=kOutput, calls=%fused_computation.4 | convolution fusion | flops 805306368 | bytes 6324228 | tf_op jit(solution)/shard_map/dot_general | solution.py:34
  43.6 5.6 %copy.52 = f32[4096,256]{1,0:T(8,128)} copy(f32[4096,256]{0,1:T(8,128)} %convolution_bitcast_fusion) | data formatting | bytes 8388608
  49.2 2.0 reshape_squeeze.10
  51.2 3.9 %convolution_bitcast_fusion.1 = f32[4096,256]{0,1:T(8,128)} fusion(f32[4096,64]{1,0:T(8,128)S(1)} %reshape_squeeze.10, bf16[1024,256]{1,0:T(8,128)(2,1)S(1)} %copy-done, s32[]{:T(128)S(6)} %select_n.57), kind=kOutput, calls=%fused_computation.5 | convolution fusion | flops 805306368 | bytes 6324228 | tf_op jit(solution)/shard_map/dot_general | solution.py:34
  55.1 5.7 %copy.51 = f32[4096,256]{1,0:T(8,128)} copy(f32[4096,256]{0,1:T(8,128)} %convolution_bitcast_fusion.1) | data formatting | bytes 8388608
  61.4 0.7 fusion.27
  62.2 225.8 %all-reduce.3.cloned.1.call-done = f32[256,256]{0,1:T(8,128)} async-done(((f32[256,256]{0,1:T(8,128)}), f32[256,256]{0,1:T(8,128)}) %all-reduce.3.cloned.1.call-update) | async-done | bytes 262160 | tf_op jit(solution)/shard_map/psum | solution.py:41
  288.0 1.3 convolution_multiply_fusion
  289.3 0.1 copy.21
  289.5 11.7 %cholesky.50 = f32[128,128]{1,0:T(8,128)S(1)} custom-call(f32[128,128]{1,0:T(8,128)S(1)} %cholesky.118), custom_call_target="Cholesky" | custom-call | tf_op jit(solution)/shard_map/jit(cholesky)/cholesky | solution.py:44
  301.2 9.8 %custom-call.18 = f32[1,128,128]{1,2,0:T(8,128)S(1)} custom-call(f32[1,128,128]{2,1,0:T(8,128)S(1)} %get-tuple-element.32), custom_call_target="InvertDiagBlocksLowerTriangular" | custom-call | tf_op jit(solution)/shard_map/jit(cholesky)/cholesky | solution.py:44
  311.1 0.2 constant_dynamic-update-slice_fusion
  311.3 0.3 convolution_subtract_fusion
  311.5 11.7 %cholesky.105 = f32[128,128]{1,0:T(8,128)S(1)} custom-call(f32[128,128]{1,0:T(8,128)S(1)} %convolution_subtract_fusion), custom_call_target="Cholesky" | custom-call | tf_op jit(solution)/shard_map/jit(cholesky)/cholesky | solution.py:44
  323.3 0.7 compare_reduce_fusion
  325.3 3.6 gather_fusion.1
  328.9 0.1 select_select_fusion.1
  329.0 3.0 multiply_reduce_fusion.2
  332.1 0.1 copy.35
  332.2 4.9 %multiply_reduce_fusion = (f32[256,64]{0,1:T(8,128)S(1)}, f32[256,64]{0,1:T(8,128)S(1)}) fusion(f32[256,64]{0,1:T(8,128)S(1)} %get-tuple-element.26, f32[4096,256]{1,0:T(8,128)} %copy.52, f32[4096,256]{1,0:T(8,128)} %copy.51, f32[256,64]{0,1:T(8,128)S(1)} %get-tuple-element.27), kind=kLoop, calls=%fused_computation.7 | loop fusion | flops 4161536 | bytes 8650752
  337.2 0.1 copy.49
  337.3 1.9 add_bitcast_fusion
  339.2 0.7 copy.53
  340.0 3.8 %while.1 = (s32[]{:T(128)}, f32[256,256]{1,0:T(8,128)S(1)}, s32[2,2]{1,0:T(2,128)S(1)}, f32[2,128,128]{2,1,0:T(8,128)S(1)}, s32[]{:T(128)}) while((s32[]{:T(128)}, f32[256,256]{1,0:T(8,128)S(1)}, s32[2,2]{1,0:T(2,128)S(1)}, f32[2,128,128]{2,1,0:T(8,128)S(1)}, s32[]{:T(128)}) %tuple.33), condition=%wide.while_cond, body=%wide.while_body.sunk | while | flops 2 | bytes 131189 | solution.py:45
  340.0 0.6 fusion.44
  340.6 1.3 bitcast_dynamic-update-slice_fusion.2
  341.9 0.6 fusion.44
  342.5 1.3 bitcast_dynamic-update-slice_fusion.2
  343.8 19.7 %custom-call.19 = f32[2,128,128]{1,2,0:T(8,128)S(1)} custom-call(f32[2,128,128]{2,1,0:T(8,128)S(1)} %get-tuple-element.12), custom_call_target="InvertDiagBlocksLowerTriangular" | custom-call | tf_op jit(solution)/shard_map/jit(_cho_solve)/triangular_solve | solution.py:45
  363.5 0.9 fusion.5
  364.4 0.9 convolution_subtract_fusion.2
  365.2 0.2 fusion.7
  365.4 0.2 fusion.6
  365.6 0.2 convolution_subtract_fusion.1
  365.8 0.2 fusion.4
  366.0 0.7 maximum_bitcast_fusion
  (33 shorter events, 0.8 us)
Async XLA Ops:
  7.4 20.7 %copy-start = (bf16[1024,256]{1,0:T(8,128)(2,1)S(1)}, bf16[1024,256]{1,0:T(8,128)(2,1)}, u32[]{:S(2)}) copy-start(bf16[1024,256]{1,0:T(8,128)(2,1)} %param.13) | copy-start | bytes 1572868
  7.4 280.6 %all-reduce.3.cloned.1.call-start = ((), (), s32[]{:S(2)}) async-start(), calls=%async_computation.2 | async-start | bytes 524288 | tf_op jit(solution)/shard_map/psum | solution.py:41
  9.1 316.2 %all-gather.2.cloned.1.call-start = ((), (), s32[]{:S(2)}) async-start(), calls=%async_computation.3 | async-start | bytes 4227072 | tf_op jit(solution)/shard_map/all_gather | solution.py:22
  16.5 347.0 %reduce-scatter.4.cloned.1.call-start = ((), (), s32[]{:S(2)}) async-start(), calls=%async_computation.4 | async-start | bytes 81920 | tf_op jit(solution)/shard_map/reduce_scatter | solution.py:39
  55.1 6.3 %copy-start.1 = (s32[3]{0:T(128)S(1)}, s32[3]{0:T(128)}, u32[]{:S(2)}) copy-start(s32[3]{0:T(128)} %param.10) | copy-start | bytes 40
Sparse Core Ops, SparseCore 0:
  13.2 274.7 all-reduce.2
Sparse Core Ops, SparseCore 1:
  16.6 90.6 all-gather.1
  340.0 17.3 reduce-scatter.3
